TPU v7x, 256 devices: a whole 4x4x8 slice. The times are simulated.
256 devices in a mesh: row: 16 (over z_hi, x, core), col: 16 (over z_lo, y).
Axes of the slice: x: 4, y: 4, z: 8 (z_hi: 2, z_lo: 4; z = z_hi * 4 + z_lo), core: 2. Of those that a mesh axis runs over, the one named last changes fastest.
Arguments:
- features: bfloat16 [64, 512, 2048], P(None, 'row', 'col'), may hold values from -6 to 6
- patch_index: int32 [512, 2048], P('row', 'col'), may hold values from 0 to 2047
- confidence: float32 [512, 2048], P('row', 'col'), may hold values from 0.2 to 1
- bank: bfloat16 [256, 576, 2048], P(('row', 'col')), may hold values from -6 to 6
- page_owner: int32 [2], replicated, may hold values from 0 to 255
- texture_weight: bfloat16 [64, 576], replicated, may hold values from -0.25 to 0.25
- conv_weight: bfloat16 [8, 9, 64, 64], replicated, may hold values from -0.25 to 0.25
Outputs:
- restored: bfloat16 [64, 512, 2048], P(None, 'row', 'col')
Inputs may be any that keep to these rules, and one draw needn't show every extreme that they name: `patch_index`: each entry is a patch number of the page. `page_owner`: each entry is a slot number.
All inputs are finite; a program needn't handle non-finite values.
Results may differ from a plain program's by a relative error of at most 0.024.
Values may be sent and summed in bfloat16 or wider, within the bound.
No kernel may reach another device: no remote copies, remote signals or barrier semaphores. Data moves between devices by JAX's collectives and lax.ppermute only.
A program may use at most 128 MiB of HBM per device.

v0:
```python
import jax
import jax.numpy as jnp
from jax import lax
from jax.sharding import PartitionSpec as P

LAYERS = 8
STEPS = 2


def with_halo(block, sides, width):
    for axis, dim in sides:
        count = lax.axis_size(axis)
        forward = [(i, i + 1) for i in range(count - 1)]
        backward = [(target, source) for source, target in forward]
        low = lax.ppermute(
            lax.slice_in_dim(block, block.shape[dim] - width, None, axis=dim), axis, forward
        )
        high = lax.ppermute(lax.slice_in_dim(block, 0, width, axis=dim), axis, backward)
        block = jnp.concatenate([low, block, high], axis=dim)
    return block


def broadcast(value, axis, root):
    mine = lax.axis_index(axis) == root
    return lax.psum(jnp.where(mine, value, jnp.zeros_like(value)), axis)


def valid_conv(padded, kernel):
    height = padded.shape[1] - 2
    width = padded.shape[2] - 2
    chans = padded.shape[0]
    windows = [
        padded[:, tap // 3 : tap // 3 + height, tap % 3 : tap % 3 + width] for tap in range(9)
    ]
    stacked = jnp.concatenate(windows, axis=0)
    flat_kernel = kernel.transpose(1, 0, 2).reshape(kernel.shape[1], 9 * chans)
    return jnp.einsum("ok,khw->ohw", flat_kernel, stacked, preferred_element_type=jnp.float32)


def with_rims(field):
    return with_halo(field, (("row", 1), ("col", 2)), 1)


def body(features, patch_index, confidence, bank, page_owner, texture_weight, conv_weight):
    tile_h = features.shape[1]
    tile_w = features.shape[2]
    flat_index = patch_index.reshape(-1)
    state = features
    for step in range(STEPS):
        owner = page_owner[step]
        local_proj = jnp.dot(texture_weight, bank[0], preferred_element_type=jnp.float32).astype(
            jnp.bfloat16
        )
        projected = broadcast(local_proj, ("row", "col"), owner)
        texture = jnp.take(projected, flat_index, axis=1).reshape(
            projected.shape[0], tile_h, tile_w
        )
        state = (state.astype(jnp.float32) + confidence[None] * texture.astype(jnp.float32)).astype(
            jnp.bfloat16
        )
        for block in range(LAYERS // 2):
            padded = with_rims(state)
            inner = jnp.maximum(valid_conv(padded, conv_weight[2 * block]), 0.0).astype(
                jnp.bfloat16
            )
            inner = with_rims(inner)
            state = (
                state.astype(jnp.float32) + valid_conv(inner, conv_weight[2 * block + 1])
            ).astype(jnp.bfloat16)
    return state


def solution(mesh):
    return jax.shard_map(
        body,
        mesh=mesh,
        in_specs=(
            P(None, "row", "col"),
            P("row", "col"),
            P("row", "col"),
            P(("row", "col"), None, None),
            P(),
            P(),
            P(),
        ),
        out_specs=P(None, "row", "col"),
        check_vma=False,
    )
```

profile of v0, /device:TPU:39, one launch (start us, length us, event | category | flops | bytes accessed | tf_op | source)
XLA Modules:
  0.0 758.1 jit_solution(7818679904812728481)
XLA Ops:
  9.2 2.3 broadcast_select_fusion
  11.6 258.3 %all-reduce.3.cloned.1.call-done = (bf16[64,2048]{1,0:T(8,128)(2,1)}, bf16[64,2048]{1,0:T(8,128)(2,1)}) async-done(((bf16[64,2048]{1,0:T(8,128)(2,1)}, bf16[64,2048]{1,0:T(8,128)(2,1)}), (bf16[64,2048]{1,0:T(8,128)(2,1)}, bf16[64,2048]{1,0:T(8,128)(2,1)})) %all-reduce.3.cloned.1.call-update) | async-done | bytes 524304 | tf_op jit(solution)/shard_map/psum | solution.py:25
  271.1 12.1 %gather_fusion = bf16[4096,64]{1,0:T(8,128)(2,1)S(1)} fusion(bf16[64,2048]{0,1:T(8,128)(2,1)S(1)} %copy.149, s32[4096]{0:T(1024)S(1)} %fusion.74), kind=kCustom, calls=%fused_computation.clone | custom fusion | bytes 1064960 | tf_op jit(solution)/shard_map/jit(_take)/gather | solution.py:55
  283.9 12.1 %gather_fusion.1 = bf16[4096,64]{1,0:T(8,128)(2,1)S(1)} fusion(bf16[64,2048]{0,1:T(8,128)(2,1)S(1)} %copy.200, s32[4096]{0:T(1024)S(1)} %fusion.74), kind=kCustom, calls=%fused_computation.1.clone | custom fusion | bytes 1064960 | tf_op jit(solution)/shard_map/jit(_take)/gather | solution.py:55
  297.4 4.6 collective-permute-start
  304.0 9.1 %collective-permute-done.1 = bf16[64,1,128]{2,0,1:T(8,128)(2,1)S(1)} collective-permute-done((bf16[64,1,128]{2,0,1:T(8,128)(2,1)S(1)}, bf16[64,1,128]{2,0,1:T(8,128)(2,1)S(1)}, u32[]{:S(2)}, u32[]{:S(2)}) %collective-permute-start.1) | collective-permute-done | bytes 16416 | tf_op jit(solution)/shard_map/ppermute | solution.py:18
  314.1 3.2 collective-permute-start.2
  317.4 6.1 collective-permute-start.3
  323.5 2.3 slice_bitcast_fusion
  334.5 9.1 %collective-permute-done.5 = bf16[64,1,128]{2,0,1:T(8,128)(2,1)S(1)} collective-permute-done((bf16[64,1,128]{2,0,1:T(8,128)(2,1)S(1)}, bf16[64,1,128]{2,0,1:T(8,128)(2,1)S(1)}, u32[]{:S(2)}, u32[]{:S(2)}) %collective-permute-start.5) | collective-permute-done | bytes 16416 | tf_op jit(solution)/shard_map/ppermute | solution.py:18
  344.2 4.8 collective-permute-start.7
  352.7 3.2 collective-permute-done.6
  359.7 3.4 collective-permute-start.8
  363.0 2.5 collective-permute-start.9
  365.6 8.8 %collective-permute-done.9 = bf16[64,1,128]{2,0,1:T(8,128)(2,1)S(1)} collective-permute-done((bf16[64,1,128]{2,0,1:T(8,128)(2,1)S(1)}, bf16[64,1,128]{2,0,1:T(8,128)(2,1)S(1)}, u32[]{:S(2)}, u32[]{:S(2)}) %collective-permute-start.9) | collective-permute-done | bytes 16416 | tf_op jit(solution)/shard_map/ppermute | solution.py:18
  377.3 3.4 collective-permute-start.10
  387.7 3.0 collective-permute-start.12
  392.6 9.3 %collective-permute-done.13 = bf16[64,1,128]{2,0,1:T(8,128)(2,1)S(1)} collective-permute-done((bf16[64,1,128]{2,0,1:T(8,128)(2,1)S(1)}, bf16[64,1,128]{2,0,1:T(8,128)(2,1)S(1)}, u32[]{:S(2)}, u32[]{:S(2)}) %collective-permute-start.13) | collective-permute-done | bytes 16416 | tf_op jit(solution)/shard_map/ppermute | solution.py:18
  404.7 3.4 collective-permute-start.14
  415.1 3.0 collective-permute-start.16
  420.2 9.3 %collective-permute-done.17 = bf16[64,1,128]{2,0,1:T(8,128)(2,1)S(1)} collective-permute-done((bf16[64,1,128]{2,0,1:T(8,128)(2,1)S(1)}, bf16[64,1,128]{2,0,1:T(8,128)(2,1)S(1)}, u32[]{:S(2)}, u32[]{:S(2)}) %collective-permute-start.17) | collective-permute-done | bytes 16416 | tf_op jit(solution)/shard_map/ppermute | solution.py:18
  432.4 3.5 collective-permute-start.18
  444.5 3.4 collective-permute-start.20
  449.8 9.3 %collective-permute-done.21 = bf16[64,1,128]{2,0,1:T(8,128)(2,1)S(1)} collective-permute-done((bf16[64,1,128]{2,0,1:T(8,128)(2,1)S(1)}, bf16[64,1,128]{2,0,1:T(8,128)(2,1)S(1)}, u32[]{:S(2)}, u32[]{:S(2)}) %collective-permute-start.21) | collective-permute-done | bytes 16416 | tf_op jit(solution)/shard_map/ppermute | solution.py:18
  462.0 3.4 collective-permute-start.22
  472.4 3.0 collective-permute-start.24
  477.4 9.3 %collective-permute-done.25 = bf16[64,1,128]{2,0,1:T(8,128)(2,1)S(1)} collective-permute-done((bf16[64,1,128]{2,0,1:T(8,128)(2,1)S(1)}, bf16[64,1,128]{2,0,1:T(8,128)(2,1)S(1)}, u32[]{:S(2)}, u32[]{:S(2)}) %collective-permute-start.25) | collective-permute-done | bytes 16416 | tf_op jit(solution)/shard_map/ppermute | solution.py:18
  489.6 3.3 collective-permute-start.26
  493.5 2.6 collective-permute-done.26
  499.9 3.5 collective-permute-start.28
  505.4 9.3 %collective-permute-done.29 = bf16[64,1,128]{2,0,1:T(8,128)(2,1)S(1)} collective-permute-done((bf16[64,1,128]{2,0,1:T(8,128)(2,1)S(1)}, bf16[64,1,128]{2,0,1:T(8,128)(2,1)S(1)}, u32[]{:S(2)}, u32[]{:S(2)}) %collective-permute-start.29) | collective-permute-done | bytes 16416 | tf_op jit(solution)/shard_map/ppermute | solution.py:18
  517.6 3.4 collective-permute-start.30
  528.0 3.0 collective-permute-start.32
  532.9 9.3 %collective-permute-done.33 = bf16[64,1,128]{2,0,1:T(8,128)(2,1)S(1)} collective-permute-done((bf16[64,1,128]{2,0,1:T(8,128)(2,1)S(1)}, bf16[64,1,128]{2,0,1:T(8,128)(2,1)S(1)}, u32[]{:S(2)}, u32[]{:S(2)}) %collective-permute-start.33) | collective-permute-done | bytes 16416 | tf_op jit(solution)/shard_map/ppermute | solution.py:18
  545.2 3.3 collective-permute-start.34
  548.9 2.8 collective-permute-done.34
  555.6 3.4 collective-permute-start.36
  560.9 9.3 %collective-permute-done.37 = bf16[64,1,128]{2,0,1:T(8,128)(2,1)S(1)} collective-permute-done((bf16[64,1,128]{2,0,1:T(8,128)(2,1)S(1)}, bf16[64,1,128]{2,0,1:T(8,128)(2,1)S(1)}, u32[]{:S(2)}, u32[]{:S(2)}) %collective-permute-start.37) | collective-permute-done | bytes 16416 | tf_op jit(solution)/shard_map/ppermute | solution.py:18
  573.0 3.8 collective-permute-start.38
  577.2 2.4 collective-permute-done.38
  583.4 3.0 collective-permute-start.40
  588.3 9.3 %collective-permute-done.41 = bf16[64,1,128]{2,0,1:T(8,128)(2,1)S(1)} collective-permute-done((bf16[64,1,128]{2,0,1:T(8,128)(2,1)S(1)}, bf16[64,1,128]{2,0,1:T(8,128)(2,1)S(1)}, u32[]{:S(2)}, u32[]{:S(2)}) %collective-permute-start.41) | collective-permute-done | bytes 16416 | tf_op jit(solution)/shard_map/ppermute | solution.py:18
  600.4 3.4 collective-permute-start.42
  604.2 2.8 collective-permute-done.42
  610.8 3.0 collective-permute-start.44
  615.7 9.3 %collective-permute-done.45 = bf16[64,1,128]{2,0,1:T(8,128)(2,1)S(1)} collective-permute-done((bf16[64,1,128]{2,0,1:T(8,128)(2,1)S(1)}, bf16[64,1,128]{2,0,1:T(8,128)(2,1)S(1)}, u32[]{:S(2)}, u32[]{:S(2)}) %collective-permute-start.45) | collective-permute-done | bytes 16416 | tf_op jit(solution)/shard_map/ppermute | solution.py:18
  627.9 3.4 collective-permute-start.46
  631.6 2.8 collective-permute-done.46
  638.3 3.0 collective-permute-start.48
  643.4 9.1 %collective-permute-done.49 = bf16[64,1,128]{2,0,1:T(8,128)(2,1)S(1)} collective-permute-done((bf16[64,1,128]{2,0,1:T(8,128)(2,1)S(1)}, bf16[64,1,128]{2,0,1:T(8,128)(2,1)S(1)}, u32[]{:S(2)}, u32[]{:S(2)}) %collective-permute-start.49) | collective-permute-done | bytes 16416 | tf_op jit(solution)/shard_map/ppermute | solution.py:18
  655.4 3.4 collective-permute-start.50
  659.1 2.8 collective-permute-done.50
  665.8 3.0 collective-permute-start.52
  670.7 9.3 %collective-permute-done.53 = bf16[64,1,128]{2,0,1:T(8,128)(2,1)S(1)} collective-permute-done((bf16[64,1,128]{2,0,1:T(8,128)(2,1)S(1)}, bf16[64,1,128]{2,0,1:T(8,128)(2,1)S(1)}, u32[]{:S(2)}, u32[]{:S(2)}) %collective-permute-start.53) | collective-permute-done | bytes 16416 | tf_op jit(solution)/shard_map/ppermute | solution.py:18
  682.8 3.4 collective-permute-start.54
  686.6 2.8 collective-permute-done.54
  693.2 3.0 collective-permute-start.56
  698.1 9.3 %collective-permute-done.57 = bf16[64,1,128]{2,0,1:T(8,128)(2,1)S(1)} collective-permute-done((bf16[64,1,128]{2,0,1:T(8,128)(2,1)S(1)}, bf16[64,1,128]{2,0,1:T(8,128)(2,1)S(1)}, u32[]{:S(2)}, u32[]{:S(2)}) %collective-permute-start.57) | collective-permute-done | bytes 16416 | tf_op jit(solution)/shard_map/ppermute | solution.py:18
  710.3 3.6 collective-permute-start.58
  714.3 2.6 collective-permute-done.58
  722.4 3.0 collective-permute-start.60
  727.3 9.3 %collective-permute-done.61 = bf16[64,1,128]{2,0,1:T(8,128)(2,1)S(1)} collective-permute-done((bf16[64,1,128]{2,0,1:T(8,128)(2,1)S(1)}, bf16[64,1,128]{2,0,1:T(8,128)(2,1)S(1)}, u32[]{:S(2)}, u32[]{:S(2)}) %collective-permute-start.61) | collective-permute-done | bytes 16416 | tf_op jit(solution)/shard_map/ppermute | solution.py:18
  739.5 3.4 collective-permute-start.62
  743.2 2.8 collective-permute-done.62
  (423 shorter events, 166.3 us)
Async XLA Ops:
  6.5 263.4 %all-reduce.3.cloned.1.call-start = ((), (), s32[]{:S(2)}) async-start(), calls=%async_computation | async-start | bytes 1048576 | tf_op jit(solution)/shard_map/psum | solution.py:25
  297.4 6.6 collective-permute-start
  302.1 11.1 %collective-permute-start.1 = (bf16[64,1,128]{2,0,1:T(8,128)(2,1)S(1)}, bf16[64,1,128]{2,0,1:T(8,128)(2,1)S(1)}, u32[]{:S(2)}, u32[]{:S(2)}) collective-permute-start(bf16[64,1,128]{2,0,1:T(8,128)(2,1)S(1)} %get-tuple-element.111), channel_id=1, source_target_pairs={{16,0},{32,16},{48,32},{64,48},{80,64},{96,80},{112,96},{128,112},... | collective-permute-start | bytes 49160 | tf_op jit(solution)/shard_map/ppermute | solution.py:18
  314.1 12.2 %collective-permute-start.2 = (bf16[64,34,1]{0,1,2:T(8,128)(2,1)S(1)}, bf16[64,34,1]{0,1,2:T(8,128)(2,1)S(1)}, u32[]{:S(2)}, u32[]{:S(2)}) collective-permute-start(bf16[64,34,1]{0,1,2:T(8,128)(2,1)S(1)} %copy.152), channel_id=1, source_target_pairs={{0,1},{1,2},{2,3},{3,4},{4,5},{5,6},{6,7},{7,8},{8,9},{9,10},{10,1... | collective-permute-start | bytes 13064 | tf_op jit(solution)/shard_map/ppermute | solution.py:15
  317.4 8.5 %collective-permute-start.3 = (bf16[64,34,1]{0,1,2:T(8,128)(2,1)S(1)}, bf16[64,34,1]{0,1,2:T(8,128)(2,1)S(1)}, u32[]{:S(2)}, u32[]{:S(2)}) collective-permute-start(bf16[64,34,1]{0,1,2:T(8,128)(2,1)S(1)} %copy.154), channel_id=1, source_target_pairs={{1,0},{2,1},{3,2},{4,3},{5,4},{6,5},{7,6},{8,7},{9,8},{10,9},{11,1... | collective-permute-start | bytes 13064 | tf_op jit(solution)/shard_map/ppermute | solution.py:18
  332.3 11.2 %collective-permute-start.5 = (bf16[64,1,128]{2,0,1:T(8,128)(2,1)S(1)}, bf16[64,1,128]{2,0,1:T(8,128)(2,1)S(1)}, u32[]{:S(2)}, u32[]{:S(2)}) collective-permute-start(bf16[64,1,128]{2,0,1:T(8,128)(2,1)S(1)} %get-tuple-element.109), channel_id=1, source_target_pairs={{16,0},{32,16},{48,32},{64,48},{80,64},{96,80},{112,96},{128,112},... | collective-permute-start | bytes 49160 | tf_op jit(solution)/shard_map/ppermute | solution.py:18
  344.2 8.1 %collective-permute-start.7 = (bf16[64,34,1]{0,1,2:T(8,128)(2,1)S(1)}, bf16[64,34,1]{0,1,2:T(8,128)(2,1)S(1)}, u32[]{:S(2)}, u32[]{:S(2)}) collective-permute-start(bf16[64,34,1]{0,1,2:T(8,128)(2,1)S(1)} %copy.160), channel_id=1, source_target_pairs={{1,0},{2,1},{3,2},{4,3},{5,4},{6,5},{7,6},{8,7},{9,8},{10,9},{11,1... | collective-permute-start | bytes 13064 | tf_op jit(solution)/shard_map/ppermute | solution.py:18
  349.3 6.5 collective-permute-start.6
  359.7 5.9 collective-permute-start.8
  363.0 11.3 %collective-permute-start.9 = (bf16[64,1,128]{2,0,1:T(8,128)(2,1)S(1)}, bf16[64,1,128]{2,0,1:T(8,128)(2,1)S(1)}, u32[]{:S(2)}, u32[]{:S(2)}) collective-permute-start(bf16[64,1,128]{2,0,1:T(8,128)(2,1)S(1)} %get-tuple-element.107), channel_id=1, source_target_pairs={{16,0},{32,16},{48,32},{64,48},{80,64},{96,80},{112,96},{128,112},... | collective-permute-start | bytes 49160 | tf_op jit(solution)/shard_map/ppermute | solution.py:18
  375.0 6.4 collective-permute-start.11
  377.3 6.5 collective-permute-start.10
  387.7 4.9 collective-permute-start.12
  390.6 11.2 %collective-permute-start.13 = (bf16[64,1,128]{2,0,1:T(8,128)(2,1)S(1)}, bf16[64,1,128]{2,0,1:T(8,128)(2,1)S(1)}, u32[]{:S(2)}, u32[]{:S(2)}) collective-permute-start(bf16[64,1,128]{2,0,1:T(8,128)(2,1)S(1)} %get-tuple-element.105), channel_id=1, source_target_pairs={{16,0},{32,16},{48,32},{64,48},{80,64},{96,80},{112,96},{128,112},... | collective-permute-start | bytes 49160 | tf_op jit(solution)/shard_map/ppermute | solution.py:18
  402.5 7.3 collective-permute-start.15
  404.7 6.5 collective-permute-start.14
  415.1 5.0 collective-permute-start.16
  418.1 11.3 %collective-permute-start.17 = (bf16[64,1,128]{2,0,1:T(8,128)(2,1)S(1)}, bf16[64,1,128]{2,0,1:T(8,128)(2,1)S(1)}, u32[]{:S(2)}, u32[]{:S(2)}) collective-permute-start(bf16[64,1,128]{2,0,1:T(8,128)(2,1)S(1)} %get-tuple-element.103), channel_id=1, source_target_pairs={{16,0},{32,16},{48,32},{64,48},{80,64},{96,80},{112,96},{128,112},... | collective-permute-start | bytes 49160 | tf_op jit(solution)/shard_map/ppermute | solution.py:18
  430.1 6.6 collective-permute-start.19
  432.4 6.5 collective-permute-start.18
  444.5 5.3 collective-permute-start.20
  447.8 11.2 %collective-permute-start.21 = (bf16[64,1,128]{2,0,1:T(8,128)(2,1)S(1)}, bf16[64,1,128]{2,0,1:T(8,128)(2,1)S(1)}, u32[]{:S(2)}, u32[]{:S(2)}) collective-permute-start(bf16[64,1,128]{2,0,1:T(8,128)(2,1)S(1)} %get-tuple-element.101), channel_id=1, source_target_pairs={{16,0},{32,16},{48,32},{64,48},{80,64},{96,80},{112,96},{128,112},... | collective-permute-start | bytes 49160 | tf_op jit(solution)/shard_map/ppermute | solution.py:18
  459.7 7.3 collective-permute-start.23
  462.0 6.5 collective-permute-start.22
  472.4 5.0 collective-permute-start.24
  475.3 11.3 %collective-permute-start.25 = (bf16[64,1,128]{2,0,1:T(8,128)(2,1)S(1)}, bf16[64,1,128]{2,0,1:T(8,128)(2,1)S(1)}, u32[]{:S(2)}, u32[]{:S(2)}) collective-permute-start(bf16[64,1,128]{2,0,1:T(8,128)(2,1)S(1)} %get-tuple-element.99), channel_id=1, source_target_pairs={{16,0},{32,16},{48,32},{64,48},{80,64},{96,80},{112,96},{128,112},... | collective-permute-start | bytes 49160 | tf_op jit(solution)/shard_map/ppermute | solution.py:18
  487.3 5.8 collective-permute-start.27
  489.6 6.5 collective-permute-start.26
  499.9 5.5 collective-permute-start.28
  503.5 11.2 %collective-permute-start.29 = (bf16[64,1,128]{2,0,1:T(8,128)(2,1)S(1)}, bf16[64,1,128]{2,0,1:T(8,128)(2,1)S(1)}, u32[]{:S(2)}, u32[]{:S(2)}) collective-permute-start(bf16[64,1,128]{2,0,1:T(8,128)(2,1)S(1)} %get-tuple-element.97), channel_id=1, source_target_pairs={{16,0},{32,16},{48,32},{64,48},{80,64},{96,80},{112,96},{128,112},... | collective-permute-start | bytes 49160 | tf_op jit(solution)/shard_map/ppermute | solution.py:18
  515.4 7.3 collective-permute-start.31
  517.6 6.5 collective-permute-start.30
  528.0 4.9 collective-permute-start.32
  531.0 11.2 %collective-permute-start.33 = (bf16[64,1,128]{2,0,1:T(8,128)(2,1)S(1)}, bf16[64,1,128]{2,0,1:T(8,128)(2,1)S(1)}, u32[]{:S(2)}, u32[]{:S(2)}) collective-permute-start(bf16[64,1,128]{2,0,1:T(8,128)(2,1)S(1)} %get-tuple-element.95), channel_id=1, source_target_pairs={{16,0},{32,16},{48,32},{64,48},{80,64},{96,80},{112,96},{128,112},... | collective-permute-start | bytes 49160 | tf_op jit(solution)/shard_map/ppermute | solution.py:18
  542.9 5.6 collective-permute-start.35
  545.2 6.5 collective-permute-start.34
  555.6 5.3 collective-permute-start.36
  558.9 11.2 %collective-permute-start.37 = (bf16[64,1,128]{2,0,1:T(8,128)(2,1)S(1)}, bf16[64,1,128]{2,0,1:T(8,128)(2,1)S(1)}, u32[]{:S(2)}, u32[]{:S(2)}) collective-permute-start(bf16[64,1,128]{2,0,1:T(8,128)(2,1)S(1)} %get-tuple-element.93), channel_id=1, source_target_pairs={{16,0},{32,16},{48,32},{64,48},{80,64},{96,80},{112,96},{128,112},... | collective-permute-start | bytes 49160 | tf_op jit(solution)/shard_map/ppermute | solution.py:18
  570.8 6.0 collective-permute-start.39
  573.0 6.5 collective-permute-start.38
  583.4 4.9 collective-permute-start.40
  586.3 11.2 %collective-permute-start.41 = (bf16[64,1,128]{2,0,1:T(8,128)(2,1)S(1)}, bf16[64,1,128]{2,0,1:T(8,128)(2,1)S(1)}, u32[]{:S(2)}, u32[]{:S(2)}) collective-permute-start(bf16[64,1,128]{2,0,1:T(8,128)(2,1)S(1)} %get-tuple-element.91), channel_id=1, source_target_pairs={{16,0},{32,16},{48,32},{64,48},{80,64},{96,80},{112,96},{128,112},... | collective-permute-start | bytes 49160 | tf_op jit(solution)/shard_map/ppermute | solution.py:18
  598.2 5.6 collective-permute-start.43
  600.4 6.5 collective-permute-start.42
  610.8 4.9 collective-permute-start.44
  613.8 11.2 %collective-permute-start.45 = (bf16[64,1,128]{2,0,1:T(8,128)(2,1)S(1)}, bf16[64,1,128]{2,0,1:T(8,128)(2,1)S(1)}, u32[]{:S(2)}, u32[]{:S(2)}) collective-permute-start(bf16[64,1,128]{2,0,1:T(8,128)(2,1)S(1)} %get-tuple-element.89), channel_id=1, source_target_pairs={{16,0},{32,16},{48,32},{64,48},{80,64},{96,80},{112,96},{128,112},... | collective-permute-start | bytes 49160 | tf_op jit(solution)/shard_map/ppermute | solution.py:18
  625.7 5.6 collective-permute-start.47
  627.9 6.5 collective-permute-start.46
  638.3 5.1 collective-permute-start.48
  641.3 11.2 %collective-permute-start.49 = (bf16[64,1,128]{2,0,1:T(8,128)(2,1)S(1)}, bf16[64,1,128]{2,0,1:T(8,128)(2,1)S(1)}, u32[]{:S(2)}, u32[]{:S(2)}) collective-permute-start(bf16[64,1,128]{2,0,1:T(8,128)(2,1)S(1)} %get-tuple-element.87), channel_id=1, source_target_pairs={{16,0},{32,16},{48,32},{64,48},{80,64},{96,80},{112,96},{128,112},... | collective-permute-start | bytes 49160 | tf_op jit(solution)/shard_map/ppermute | solution.py:18
  653.1 5.6 collective-permute-start.51
  655.4 6.5 collective-permute-start.50
  665.8 4.9 collective-permute-start.52
  668.7 11.2 %collective-permute-start.53 = (bf16[64,1,128]{2,0,1:T(8,128)(2,1)S(1)}, bf16[64,1,128]{2,0,1:T(8,128)(2,1)S(1)}, u32[]{:S(2)}, u32[]{:S(2)}) collective-permute-start(bf16[64,1,128]{2,0,1:T(8,128)(2,1)S(1)} %get-tuple-element.85), channel_id=1, source_target_pairs={{16,0},{32,16},{48,32},{64,48},{80,64},{96,80},{112,96},{128,112},... | collective-permute-start | bytes 49160 | tf_op jit(solution)/shard_map/ppermute | solution.py:18
  680.6 5.6 collective-permute-start.55
  682.8 6.5 collective-permute-start.54
  693.2 4.9 collective-permute-start.56
  696.2 11.2 %collective-permute-start.57 = (bf16[64,1,128]{2,0,1:T(8,128)(2,1)S(1)}, bf16[64,1,128]{2,0,1:T(8,128)(2,1)S(1)}, u32[]{:S(2)}, u32[]{:S(2)}) collective-permute-start(bf16[64,1,128]{2,0,1:T(8,128)(2,1)S(1)} %get-tuple-element.83), channel_id=1, source_target_pairs={{16,0},{32,16},{48,32},{64,48},{80,64},{96,80},{112,96},{128,112},... | collective-permute-start | bytes 49160 | tf_op jit(solution)/shard_map/ppermute | solution.py:18
  708.1 5.8 collective-permute-start.59
  710.3 6.5 collective-permute-start.58
  722.4 4.9 collective-permute-start.60
  725.4 11.2 %collective-permute-start.61 = (bf16[64,1,128]{2,0,1:T(8,128)(2,1)S(1)}, bf16[64,1,128]{2,0,1:T(8,128)(2,1)S(1)}, u32[]{:S(2)}, u32[]{:S(2)}) collective-permute-start(bf16[64,1,128]{2,0,1:T(8,128)(2,1)S(1)} %get-tuple-element.81), channel_id=1, source_target_pairs={{16,0},{32,16},{48,32},{64,48},{80,64},{96,80},{112,96},{128,112},... | collective-permute-start | bytes 49160 | tf_op jit(solution)/shard_map/ppermute | solution.py:18
  737.2 5.6 collective-permute-start.63
  739.5 6.5 collective-permute-start.62
  (24 other events, 102.0 us)
Sparse Core Ops, SparseCore 0:
  13.0 256.9 all-reduce.2
where the time goes:
time: 769 us; the launch traced here: 758 us
  waiting for transfers between devices  440 us (57%)
  starting transfers between devices  173 us (22%)
  local copies, waits for them, and re-layouts  89.8 us (12%)
  matrix products  19.1 us (2%)
  other arithmetic  18.7 us (2%)
  between operations  17.9 us (2%)
    psum x1, waiting for transfers between devices, broadcast(): return lax.psum(jnp.where(mine, value, jnp.zeros_like(value)), axis)  258 us
    ppermute x32, waiting for transfers between devices, with_halo(): lax.ppermute(lax.slice_in_dim(block, 0, width, axis=dim), axis, backward)  147 us
    ppermute x32, starting transfers between devices, with_halo(): lax.ppermute(lax.slice_in_dim(block, block.shape[dim] - width, None, axis...  103 us
    ppermute x32, starting transfers between devices, with_halo(): lax.ppermute(lax.slice_in_dim(block, 0, width, axis=dim), axis, backward)  69.7 us
    ppermute x32, waiting for transfers between devices, with_halo(): lax.ppermute(lax.slice_in_dim(block, block.shape[dim] - width, None, axis...  34.5 us
    gather x4, local copies, waits for them, and re-layouts, body(): jnp.take(projected, flat_index, axis=1)  24.9 us
    unnamed x142, local copies, waits for them, and re-layouts  18 us
    dot_general x16, matrix products, valid_conv(): jnp.einsum('ok,khw->ohw', flat_kernel, stacked, preferred_element_type=jn...  16.8 us
  transfers between devices with their start and end apart: 65, of which 32 were waited for; matrix products, arithmetic and copies ran while one was open for 3% of the time, Pallas kernels for 0%

commit v1 on v0

v1 whole, which is shorter than its diff:
```python
import jax
import jax.numpy as jnp
from jax import lax
from jax.sharding import PartitionSpec as P

LAYERS = 8
STEPS = 2
HALO = LAYERS


def shift_pairs(n_row, n_col, dr, dc):
    pairs = []
    for r in range(n_row):
        for c in range(n_col):
            tr, tc = r + dr, c + dc
            if 0 <= tr < n_row and 0 <= tc < n_col:
                pairs.append((r * n_col + c, tr * n_col + tc))
    return pairs


def exchange(block, width):
    n_row = lax.axis_size("row")
    n_col = lax.axis_size("col")
    axes = ("row", "col")
    rows = {-1: slice(block.shape[1] - width, None), 0: slice(None), 1: slice(0, width)}
    cols = {-1: slice(block.shape[2] - width, None), 0: slice(None), 1: slice(0, width)}
    got = {}
    for dr in (-1, 0, 1):
        for dc in (-1, 0, 1):
            if dr == 0 and dc == 0:
                continue
            piece = block[:, rows[dr], cols[dc]]
            got[(dr, dc)] = lax.ppermute(piece, axes, shift_pairs(n_row, n_col, -dr, -dc))
    top = jnp.concatenate([got[(-1, -1)], got[(-1, 0)], got[(-1, 1)]], axis=2)
    mid = jnp.concatenate([got[(0, -1)], block, got[(0, 1)]], axis=2)
    bot = jnp.concatenate([got[(1, -1)], got[(1, 0)], got[(1, 1)]], axis=2)
    return jnp.concatenate([top, mid, bot], axis=1)


def broadcast_pages(masked):
    axes = ("row", "col")
    n = lax.axis_size("row") * lax.axis_size("col")
    steps, chans, width = masked.shape
    chunks = masked.reshape(steps, chans, n, width // n).transpose(2, 0, 1, 3)
    mine = lax.all_to_all(chunks, axes, 0, 0, tiled=True)
    total = jnp.sum(mine.astype(jnp.float32), axis=0).astype(masked.dtype)
    spread = jnp.broadcast_to(total[None], (n,) + total.shape)
    back = lax.all_to_all(spread, axes, 0, 0, tiled=True)
    return back.transpose(1, 2, 0, 3).reshape(steps, chans, width)


def conv_valid(field, kernel):
    taps = kernel.reshape(3, 3, kernel.shape[1], kernel.shape[2]).transpose(2, 3, 0, 1)
    out = lax.conv_general_dilated(
        field[None],
        taps,
        (1, 1),
        "VALID",
        dimension_numbers=("NCHW", "OIHW", "NCHW"),
        preferred_element_type=jnp.float32,
    )
    return out[0]


def body(features, patch_index, confidence, bank, page_owner, texture_weight, conv_weight):
    chans, tile_h, tile_w = features.shape
    n_row = lax.axis_size("row")
    n_col = lax.axis_size("col")
    r = lax.axis_index("row")
    c = lax.axis_index("col")
    me = r * n_col + c

    local_proj = jnp.dot(texture_weight, bank[0], preferred_element_type=jnp.float32).astype(jnp.bfloat16)
    masked = jnp.stack(
        [jnp.where(me == page_owner[s], local_proj, jnp.zeros_like(local_proj)) for s in range(STEPS)]
    )
    pages = broadcast_pages(masked)

    ext_rows = r * tile_h - HALO + jnp.arange(tile_h + 2 * HALO)
    ext_cols = c * tile_w - HALO + jnp.arange(tile_w + 2 * HALO)
    row_ok = (ext_rows >= 0) & (ext_rows < n_row * tile_h)
    col_ok = (ext_cols >= 0) & (ext_cols < n_col * tile_w)
    valid = row_ok[:, None] & col_ok[None, :]

    flat_index = patch_index.reshape(-1)
    state = features
    for step in range(STEPS):
        page_rows = pages[step].T
        texture = page_rows[flat_index].T.reshape(chans, tile_h, tile_w)
        state = (state.astype(jnp.float32) + confidence[None] * texture.astype(jnp.float32)).astype(jnp.bfloat16)
        x = exchange(state, HALO)
        halo = HALO
        for block in range(LAYERS // 2):
            inner = jnp.maximum(conv_valid(x, conv_weight[2 * block]), 0.0)
            halo -= 1
            keep = valid[HALO - halo : HALO + tile_h + halo, HALO - halo : HALO + tile_w + halo]
            inner = jnp.where(keep[None], inner, 0.0).astype(jnp.bfloat16)
            res = x[:, 2:-2, 2:-2].astype(jnp.float32) + conv_valid(inner, conv_weight[2 * block + 1])
            halo -= 1
            keep = valid[HALO - halo : HALO + tile_h + halo, HALO - halo : HALO + tile_w + halo]
            x = jnp.where(keep[None], res, 0.0).astype(jnp.bfloat16)
        state = x
    return state


def solution(mesh):
    return jax.shard_map(
        body,
        mesh=mesh,
        in_specs=(
            P(None, "row", "col"),
            P("row", "col"),
            P("row", "col"),
            P(("row", "col"), None, None),
            P(),
            P(),
            P(),
        ),
        out_specs=P(None, "row", "col"),
        check_vma=False,
    )
```

time: 769 us -> 451 us (0.59)
  waiting for transfers between devices: 440 us -> 69.4 us
  starting transfers between devices: 173 us -> 91 us
  local copies, waits for them, and re-layouts: 89.8 us -> 167 us
  matrix products: 19.1 us -> 57.2 us
  other arithmetic: 18.7 us -> 54.4 us
  between operations: 17.9 us -> 3.28 us
    psum x1 -> x0, waiting for transfers between devices: 258 us -> none  [broadcast(): return lax.psum(jnp.where(mine, value, jnp.zeros_like(value)), axis)]
    ppermute x64 -> x16, waiting for transfers between devices: 182 us -> 32.9 us  [exchange(): got[dr, dc] = lax.ppermute(piece, axes, shift_pairs(n_row, n_col, -dr, -dc))]
    ppermute x64 -> x16, starting transfers between devices: 173 us -> 68.2 us  [exchange(): got[dr, dc] = lax.ppermute(piece, axes, shift_pairs(n_row, n_col, -dr, -dc))]
    conv_general_dilated x0 -> x16, matrix products: none -> 55.7 us  [conv_valid(): lax.conv_general_dilated(field[None], taps, (1, 1), 'VALID', dimension_nu...]
    unnamed x142 -> x89, local copies, waits for them, and re-layouts: 18 us -> 72.5 us
    convert_element_type x0 -> x17, other arithmetic: none -> 46.5 us  [the longest x7 27.8 us: body(): x = jnp.where(keep[None], res, 0.0).astype(jnp.bfloat16)]
    all_to_all x0 -> x2, waiting for transfers between devices: none -> 36.5 us  [the longest x1 18.8 us: broadcast_pages(): mine = lax.all_to_all(chunks, axes, 0, 0, tiled=True)]
    conv_general_dilated x0 -> x48, local copies, waits for them, and re-layouts: none -> 29.9 us  [conv_valid(): lax.conv_general_dilated(field[None], taps, (1, 1), 'VALID', dimension_nu...]
  transfers between devices with their start and end apart: 65 -> 18, of which waited for: 32 -> 5; matrix products, arithmetic and copies ran while one was open for 3% -> 4% of each run, Pallas kernels for 0% -> 0%
where the time goes in v1:
time: 451 us; the launch traced here: 442 us
  local copies, waits for them, and re-layouts  167 us (37%)
  starting transfers between devices  91 us (20%)
  waiting for transfers between devices  69.4 us (15%)
  matrix products  57.2 us (13%)
  other arithmetic  54.4 us (12%)
    unnamed x89, local copies, waits for them, and re-layouts  72.5 us
    ppermute x16, starting transfers between devices, exchange(): got[dr, dc] = lax.ppermute(piece, axes, shift_pairs(n_row, n_col, -dr, -dc))  68.2 us
    conv_general_dilated x16, matrix products, conv_valid(): lax.conv_general_dilated(field[None], taps, (1, 1), 'VALID', dimension_nu...  55.7 us
    ppermute x16, waiting for transfers between devices, exchange(): got[dr, dc] = lax.ppermute(piece, axes, shift_pairs(n_row, n_col, -dr, -dc))  32.9 us
    conv_general_dilated x48, local copies, waits for them, and re-layouts, conv_valid(): lax.conv_general_dilated(field[None], taps, (1, 1), 'VALID', dimension_nu...  29.9 us
    convert_element_type x7, other arithmetic, body(): x = jnp.where(keep[None], res, 0.0).astype(jnp.bfloat16)  27.8 us
    gather x2, local copies, waits for them, and re-layouts, body(): texture = page_rows[flat_index].T.reshape(chans, tile_h, tile_w)  24.3 us
    all_to_all x1, waiting for transfers between devices, broadcast_pages(): mine = lax.all_to_all(chunks, axes, 0, 0, tiled=True)  18.8 us
  transfers between devices with their start and end apart: 18, of which 5 were waited for; matrix products, arithmetic and copies ran while one was open for 4% of the time, Pallas kernels for 0%

profile of v1, /device:TPU:39, one launch (start us, length us, event | category | flops | bytes accessed | tf_op | source)
XLA Modules:
  0.0 442.1 jit_solution(2563933201384799338)
XLA Ops:
  6.4 14.6 %all-to-all-start = ((bf16[256,2,512]{2,1,0:T(2,128)(2,1)}), bf16[256,2,512]{2,1,0:T(2,128)(2,1)S(1)}, u32[]{:S(2)}, u32[]{:S(2)}) async-start(bf16[256,2,512]{2,1,0:T(2,128)(2,1)} %reshape.278), calls=%async_computation | async-start | bytes 1048576 | tf_op jit(solution)/shard_map/all_to_all | solution.py:45
  21.1 18.8 %all-to-all-done = bf16[256,2,512]{2,1,0:T(2,128)(2,1)S(1)} async-done(((bf16[256,2,512]{2,1,0:T(2,128)(2,1)}), bf16[256,2,512]{2,1,0:T(2,128)(2,1)S(1)}, u32[]{:S(2)}, u32[]{:S(2)}) %all-to-all-start) | async-done | bytes 524320 | tf_op jit(solution)/shard_map/all_to_all | solution.py:45
  42.3 8.2 %all-to-all-start.1 = ((bf16[256,2,512]{2,1,0:T(2,128)(2,1)}), bf16[256,2,512]{2,1,0:T(2,128)(2,1)S(1)}, u32[]{:S(2)}, u32[]{:S(2)}) async-start(bf16[256,2,512]{2,1,0:T(2,128)(2,1)} %reshape.280), calls=%async_computation.1 | async-start | bytes 1048576 | tf_op jit(solution)/shard_map/all_to_all | solution.py:48
  51.7 17.7 %all-to-all-done.1 = bf16[256,2,512]{2,1,0:T(2,128)(2,1)S(1)} async-done(((bf16[256,2,512]{2,1,0:T(2,128)(2,1)}), bf16[256,2,512]{2,1,0:T(2,128)(2,1)S(1)}, u32[]{:S(2)}, u32[]{:S(2)}) %all-to-all-start.1) | async-done | bytes 524320 | tf_op jit(solution)/shard_map/all_to_all | solution.py:48
  70.3 12.1 %gather_fusion = bf16[4096,64]{1,0:T(8,128)(2,1)S(1)} fusion(bf16[2048,64]{1,0:T(8,128)(2,1)S(1)} %get-tuple-element.13, s32[4096]{0:T(1024)S(1)} %broadcast_clamp_fusion), kind=kCustom, calls=%fused_computation | custom fusion | bytes 1064960 | tf_op jit(solution)/shard_map/gather | solution.py:89
  83.9 2.6 copy.194
  88.7 4.8 %collective-permute-start = (bf16[64,8,8]{2,1,0:T(8,128)(2,1)S(1)}, bf16[64,8,8]{2,1,0:T(8,128)(2,1)S(1)}, u32[]{:S(2)}, u32[]{:S(2)}) collective-permute-start(bf16[64,8,8]{2,1,0:T(8,128)(2,1)S(1)} %get-tuple-element.23), channel_id=1, source_target_pairs={{0,17},{1,18},{2,19},{3,20},{4,21},{5,22},{6,23},{7,24},{8,25},{9,... | collective-permute-start | bytes 24584 | tf_op jit(solution)/shard_map/ppermute | solution.py:33
  93.5 3.6 collective-permute-start.2
  99.8 5.9 %collective-permute-start.7 = (bf16[64,8,8]{2,1,0:T(8,128)(2,1)}, bf16[64,8,8]{2,1,0:T(8,128)(2,1)}, u32[]{:S(2)}, u32[]{:S(2)}) collective-permute-start(bf16[64,8,8]{2,1,0:T(8,128)(2,1)} %get-tuple-element.24), channel_id=1, source_target_pairs={{17,0},{18,1},{19,2},{20,3},{21,4},{22,5},{23,6},{24,7},{25,8},{26... | collective-permute-start | bytes 24584 | tf_op jit(solution)/shard_map/ppermute | solution.py:33
  107.6 5.5 %collective-permute-start.4 = (bf16[64,32,8]{2,1,0:T(8,128)(2,1)}, bf16[64,32,8]{2,1,0:T(8,128)(2,1)}, u32[]{:S(2)}, u32[]{:S(2)}) collective-permute-start(bf16[64,32,8]{2,1,0:T(8,128)(2,1)} %get-tuple-element.30), channel_id=1, source_target_pairs={{1,0},{2,1},{3,2},{4,3},{5,4},{6,5},{7,6},{8,7},{9,8},{10,9},{11,1... | collective-permute-start | bytes 98312 | tf_op jit(solution)/shard_map/ppermute | solution.py:33
  113.1 9.5 %collective-permute-start.1 = (bf16[64,8,128]{2,1,0:T(8,128)(2,1)}, bf16[64,8,128]{2,1,0:T(8,128)(2,1)}, u32[]{:S(2)}, u32[]{:S(2)}) collective-permute-start(bf16[64,8,128]{2,1,0:T(8,128)(2,1)} %get-tuple-element.27), channel_id=1, source_target_pairs={{0,16},{1,17},{2,18},{3,19},{4,20},{5,21},{6,22},{7,23},{8,24},{9,... | collective-permute-start | bytes 393224 | tf_op jit(solution)/shard_map/ppermute | solution.py:33
  126.1 12.1 %gather_fusion.1 = bf16[4096,64]{1,0:T(8,128)(2,1)S(1)} fusion(bf16[2048,64]{1,0:T(8,128)(2,1)S(1)} %get-tuple-element.14, s32[4096]{0:T(1024)S(1)} %broadcast_clamp_fusion), kind=kCustom, calls=%fused_computation.1 | custom fusion | bytes 1064960 | tf_op jit(solution)/shard_map/gather | solution.py:89
  139.7 2.5 copy.195
  142.3 3.0 maximum_maximum_fusion
  145.3 3.7 copy.126
  151.3 4.1 select_maximum_fusion.1
  155.9 2.8 fusion.83
  159.9 4.1 broadcast_select_fusion.1
  167.1 5.9 %copy.196 = f32[44,1,140,64]{2,0,3,1:T(8,128)} copy(f32[44,1,140,64]{3,0,2,1:T(8,128)} %slice.248) | data formatting | bytes 3153920
  172.9 4.6 %fusion.15 = bf16[64,44,140]{2,1,0:T(8,128)(2,1)} fusion(f32[44,1,140,64]{2,0,3,1:T(8,128)} %copy.196, bf16[64,48,144]{2,1,0:T(8,128)(2,1)S(1)} %maximum_maximum_fusion, pred[44,140]{1,0:T(8,128)(4,1)S(1)} %slice.233), kind=kLoop, calls=%fused_computation.29 | loop fusion | flops 1576960 | bytes 3160080 | tf_op jit(solution)/shard_map/convert_element_type | solution.py:101
  177.5 5.5 %copy.204 = bf16[64,44,1,140]{0,1,3,2:T(8,128)(2,1)} copy(bf16[64,44,1,140]{3,1,0,2:T(8,128)(2,1)} %bitcast.266) | data formatting | bytes 1576960
  185.7 3.8 select_maximum_fusion.3
  190.0 2.3 fusion.99
  193.5 3.7 fusion.120
  199.9 5.7 %copy.197 = f32[40,1,136,64]{2,0,3,1:T(8,128)} copy(f32[40,1,136,64]{3,0,2,1:T(8,128)} %slice.254) | data formatting | bytes 2785280
  205.6 4.0 fusion.35
  209.6 4.1 copy.144
  214.6 3.2 select_maximum_fusion.5
  220.6 3.2 convolution_select_fusion.1
  225.9 5.8 %copy.198 = f32[36,1,132,64]{2,0,3,1:T(8,128)} copy(f32[36,1,132,64]{3,0,2,1:T(8,128)} %slice.260) | data formatting | bytes 2433024
  231.8 4.0 fusion.33
  235.7 5.0 %copy.205 = bf16[64,36,1,132]{0,1,3,2:T(8,128)(2,1)} copy(bf16[64,36,1,132]{3,1,0,2:T(8,128)(2,1)} %bitcast.276) | data formatting | bytes 1216512
  243.3 2.9 select_maximum_fusion.7
  249.1 2.8 convolution_select_fusion.3
  253.9 3.0 copy.199
  259.1 8.2 %collective-permute-start.10 = (bf16[64,8,8]{2,1,0:T(8,128)(2,1)S(1)}, bf16[64,8,8]{2,1,0:T(8,128)(2,1)S(1)}, u32[]{:S(2)}, u32[]{:S(2)}) collective-permute-start(bf16[64,8,8]{2,1,0:T(8,128)(2,1)S(1)} %get-tuple-element.18), channel_id=1, source_target_pairs={{1,16},{2,17},{3,18},{4,19},{5,20},{6,21},{7,22},{8,23},{9,24},{10... | collective-permute-start | bytes 24584 | tf_op jit(solution)/shard_map/ppermute | solution.py:33
  269.2 9.7 %collective-permute-start.9 = (bf16[64,8,128]{2,1,0:T(8,128)(2,1)S(1)}, bf16[64,8,128]{2,1,0:T(8,128)(2,1)S(1)}, u32[]{:S(2)}, u32[]{:S(2)}) collective-permute-start(bf16[64,8,128]{2,1,0:T(8,128)(2,1)S(1)} %get-tuple-element.19), channel_id=1, source_target_pairs={{0,16},{1,17},{2,18},{3,19},{4,20},{5,21},{6,22},{7,23},{8,24},{9,... | collective-permute-start | bytes 393224 | tf_op jit(solution)/shard_map/ppermute | solution.py:33
  279.1 4.5 %collective-permute-start.11 = (bf16[64,32,8]{2,1,0:T(8,128)(2,1)S(1)}, bf16[64,32,8]{2,1,0:T(8,128)(2,1)S(1)}, u32[]{:S(2)}, u32[]{:S(2)}) collective-permute-start(bf16[64,32,8]{2,1,0:T(8,128)(2,1)S(1)} %get-tuple-element.21), channel_id=1, source_target_pairs={{0,1},{1,2},{2,3},{3,4},{4,5},{5,6},{6,7},{7,8},{8,9},{9,10},{10,1... | collective-permute-start | bytes 98312 | tf_op jit(solution)/shard_map/ppermute | solution.py:33
  283.7 2.9 collective-permute-start.12
  288.5 14.4 %collective-permute-done.13 = bf16[64,8,8]{2,1,0:T(8,128)(2,1)S(1)} collective-permute-done((bf16[64,8,8]{2,1,0:T(8,128)(2,1)S(1)}, bf16[64,8,8]{2,1,0:T(8,128)(2,1)S(1)}, u32[]{:S(2)}, u32[]{:S(2)}) %collective-permute-start.13) | collective-permute-done | bytes 8224 | tf_op jit(solution)/shard_map/ppermute | solution.py:33
  304.8 12.0 %collective-permute-done.15 = bf16[64,8,8]{2,1,0:T(8,128)(2,1)S(1)} collective-permute-done((bf16[64,8,8]{2,1,0:T(8,128)(2,1)S(1)}, bf16[64,8,8]{2,1,0:T(8,128)(2,1)S(1)}, u32[]{:S(2)}, u32[]{:S(2)}) %collective-permute-start.15) | collective-permute-done | bytes 8224 | tf_op jit(solution)/shard_map/ppermute | solution.py:33
  318.7 6.5 %collective-permute-done.8 = bf16[64,8,8]{2,1,0:T(8,128)(2,1)S(1)} collective-permute-done((bf16[64,8,8]{2,1,0:T(8,128)(2,1)S(1)}, bf16[64,8,8]{2,1,0:T(8,128)(2,1)S(1)}, u32[]{:S(2)}, u32[]{:S(2)}) %collective-permute-start.8) | collective-permute-done | bytes 8224 | tf_op jit(solution)/shard_map/ppermute | solution.py:33
  327.3 3.7 copy.162
  333.2 4.1 select_maximum_fusion
  337.8 2.8 fusion.84
  341.9 4.1 broadcast_select_fusion
  349.0 5.9 %copy.200 = f32[44,1,140,64]{2,0,3,1:T(8,128)} copy(f32[44,1,140,64]{3,0,2,1:T(8,128)} %slice.280) | data formatting | bytes 3153920
  354.9 4.6 %fusion.13 = bf16[64,44,140]{2,1,0:T(8,128)(2,1)} fusion(f32[44,1,140,64]{2,0,3,1:T(8,128)} %copy.200, bf16[64,48,144]{2,1,0:T(8,128)(2,1)S(1)} %maximum_maximum_fusion.1, pred[44,140]{1,0:T(8,128)(4,1)S(1)} %slice.233), kind=kLoop, calls=%fused_computation.26 | loop fusion | flops 1576960 | bytes 3160080 | tf_op jit(solution)/shard_map/convert_element_type | solution.py:101
  359.4 5.5 %copy.206 = bf16[64,44,1,140]{0,1,3,2:T(8,128)(2,1)} copy(bf16[64,44,1,140]{3,1,0,2:T(8,128)(2,1)} %bitcast.265) | data formatting | bytes 1576960
  367.6 3.8 select_maximum_fusion.2
  371.9 2.3 fusion.100
  375.4 3.7 fusion.117
  381.8 5.7 %copy.201 = f32[40,1,136,64]{2,0,3,1:T(8,128)} copy(f32[40,1,136,64]{3,0,2,1:T(8,128)} %slice.285) | data formatting | bytes 2785280
  387.5 4.0 fusion.31
  391.5 4.1 copy.178
  396.5 3.2 select_maximum_fusion.4
  402.5 3.2 convolution_select_fusion
  407.8 5.8 %copy.202 = f32[36,1,132,64]{2,0,3,1:T(8,128)} copy(f32[36,1,132,64]{3,0,2,1:T(8,128)} %slice.290) | data formatting | bytes 2433024
  413.6 4.0 fusion.29
  417.6 5.0 %copy.207 = bf16[64,36,1,132]{0,1,3,2:T(8,128)(2,1)} copy(bf16[64,36,1,132]{3,1,0,2:T(8,128)(2,1)} %bitcast.275) | data formatting | bytes 1216512
  425.1 2.9 select_maximum_fusion.6
  431.1 2.8 convolution_select_fusion.2
  435.8 3.0 copy.203
  438.8 2.7 fusion.172
  (206 shorter events, 88.8 us)
Async XLA Ops:
  0.0 2.8 copy-start
  6.4 33.5 %all-to-all-start = ((bf16[256,2,512]{2,1,0:T(2,128)(2,1)}), bf16[256,2,512]{2,1,0:T(2,128)(2,1)S(1)}, u32[]{:S(2)}, u32[]{:S(2)}) async-start(bf16[256,2,512]{2,1,0:T(2,128)(2,1)} %reshape.278), calls=%async_computation | async-start | bytes 1048576 | tf_op jit(solution)/shard_map/all_to_all | solution.py:45
  40.8 9.7 %copy-start.27 = (s32[32,128]{1,0:T(8,128)S(1)}, s32[32,128]{1,0:T(8,128)}, u32[]{:S(2)}) copy-start(s32[32,128]{1,0:T(8,128)} %param.8) | copy-start | bytes 49156
  40.8 9.8 %copy-start.6 = (bf16[8,9,64,64]{3,2,1,0:T(8,128)(2,1)S(1)}, bf16[8,9,64,64]{3,2,1,0:T(8,128)(2,1)}, u32[]{:S(2)}) copy-start(bf16[8,9,64,64]{3,2,1,0:T(8,128)(2,1)} %param.13) | copy-start | bytes 1769476
  42.3 27.1 %all-to-all-start.1 = ((bf16[256,2,512]{2,1,0:T(2,128)(2,1)}), bf16[256,2,512]{2,1,0:T(2,128)(2,1)S(1)}, u32[]{:S(2)}, u32[]{:S(2)}) async-start(bf16[256,2,512]{2,1,0:T(2,128)(2,1)} %reshape.280), calls=%async_computation.1 | async-start | bytes 1048576 | tf_op jit(solution)/shard_map/all_to_all | solution.py:48
  83.9 2.6 copy-start.7
  83.9 2.6 copy-start.26
  88.7 18.9 %collective-permute-start = (bf16[64,8,8]{2,1,0:T(8,128)(2,1)S(1)}, bf16[64,8,8]{2,1,0:T(8,128)(2,1)S(1)}, u32[]{:S(2)}, u32[]{:S(2)}) collective-permute-start(bf16[64,8,8]{2,1,0:T(8,128)(2,1)S(1)} %get-tuple-element.23), channel_id=1, source_target_pairs={{0,17},{1,18},{2,19},{3,20},{4,21},{5,22},{6,23},{7,24},{8,25},{9,... | collective-permute-start | bytes 24584 | tf_op jit(solution)/shard_map/ppermute | solution.py:33
  93.5 19.6 %collective-permute-start.2 = (bf16[64,8,8]{2,1,0:T(8,128)(2,1)S(1)}, bf16[64,8,8]{2,1,0:T(8,128)(2,1)S(1)}, u32[]{:S(2)}, u32[]{:S(2)}) collective-permute-start(bf16[64,8,8]{2,1,0:T(8,128)(2,1)S(1)} %get-tuple-element.26), channel_id=1, source_target_pairs={{1,16},{2,17},{3,18},{4,19},{5,20},{6,21},{7,22},{8,23},{9,24},{10... | collective-permute-start | bytes 24584 | tf_op jit(solution)/shard_map/ppermute | solution.py:33
  97.1 25.5 %collective-permute-start.5 = (bf16[64,8,8]{2,1,0:T(8,128)(2,1)S(1)}, bf16[64,8,8]{2,1,0:T(8,128)(2,1)S(1)}, u32[]{:S(2)}, u32[]{:S(2)}) collective-permute-start(bf16[64,8,8]{2,1,0:T(8,128)(2,1)S(1)} %get-tuple-element.25), channel_id=1, source_target_pairs={{16,1},{17,2},{18,3},{19,4},{20,5},{21,6},{22,7},{23,8},{24,9},{25... | collective-permute-start | bytes 24584 | tf_op jit(solution)/shard_map/ppermute | solution.py:33
  99.8 42.5 %collective-permute-start.7 = (bf16[64,8,8]{2,1,0:T(8,128)(2,1)}, bf16[64,8,8]{2,1,0:T(8,128)(2,1)}, u32[]{:S(2)}, u32[]{:S(2)}) collective-permute-start(bf16[64,8,8]{2,1,0:T(8,128)(2,1)} %get-tuple-element.24), channel_id=1, source_target_pairs={{17,0},{18,1},{19,2},{20,3},{21,4},{22,5},{23,6},{24,7},{25,8},{26... | collective-permute-start | bytes 24584 | tf_op jit(solution)/shard_map/ppermute | solution.py:33
  105.7 36.6 %collective-permute-start.3 = (bf16[64,32,8]{2,1,0:T(8,128)(2,1)}, bf16[64,32,8]{2,1,0:T(8,128)(2,1)}, u32[]{:S(2)}, u32[]{:S(2)}) collective-permute-start(bf16[64,32,8]{2,1,0:T(8,128)(2,1)} %get-tuple-element.29), channel_id=1, source_target_pairs={{0,1},{1,2},{2,3},{3,4},{4,5},{5,6},{6,7},{7,8},{8,9},{9,10},{10,1... | collective-permute-start | bytes 98312 | tf_op jit(solution)/shard_map/ppermute | solution.py:33
  107.6 34.7 %collective-permute-start.4 = (bf16[64,32,8]{2,1,0:T(8,128)(2,1)}, bf16[64,32,8]{2,1,0:T(8,128)(2,1)}, u32[]{:S(2)}, u32[]{:S(2)}) collective-permute-start(bf16[64,32,8]{2,1,0:T(8,128)(2,1)} %get-tuple-element.30), channel_id=1, source_target_pairs={{1,0},{2,1},{3,2},{4,3},{5,4},{6,5},{7,6},{8,7},{9,8},{10,9},{11,1... | collective-permute-start | bytes 98312 | tf_op jit(solution)/shard_map/ppermute | solution.py:33
  113.1 9.5 %copy-start.24 = (bf16[64,8,8]{2,1,0:T(8,128)(2,1)}, bf16[64,8,8]{2,1,0:T(8,128)(2,1)S(1)}, u32[]{:S(2)}) copy-start(bf16[64,8,8]{2,1,0:T(8,128)(2,1)S(1)} %collective-permute-done.2) | copy-start | bytes 24580
  113.1 29.2 %collective-permute-start.1 = (bf16[64,8,128]{2,1,0:T(8,128)(2,1)}, bf16[64,8,128]{2,1,0:T(8,128)(2,1)}, u32[]{:S(2)}, u32[]{:S(2)}) collective-permute-start(bf16[64,8,128]{2,1,0:T(8,128)(2,1)} %get-tuple-element.27), channel_id=1, source_target_pairs={{0,16},{1,17},{2,18},{3,19},{4,20},{5,21},{6,22},{7,23},{8,24},{9,... | collective-permute-start | bytes 393224 | tf_op jit(solution)/shard_map/ppermute | solution.py:33
  122.6 3.5 copy-start.25
  122.6 19.7 %collective-permute-start.6 = (bf16[64,8,128]{2,1,0:T(8,128)(2,1)}, bf16[64,8,128]{2,1,0:T(8,128)(2,1)}, u32[]{:S(2)}, u32[]{:S(2)}) collective-permute-start(bf16[64,8,128]{2,1,0:T(8,128)(2,1)} %get-tuple-element.28), channel_id=1, source_target_pairs={{16,0},{17,1},{18,2},{19,3},{20,4},{21,5},{22,6},{23,7},{24,8},{25... | collective-permute-start | bytes 393224 | tf_op jit(solution)/shard_map/ppermute | solution.py:33
  149.0 2.3 copy-start.22
  149.0 2.3 copy-start.35
  159.0 0.9 copy-start.20
  159.0 0.9 copy-start.34
  184.8 0.9 copy-start.18
  184.8 0.9 copy-start.33
  192.6 0.9 copy-start.16
  192.6 0.9 copy-start.32
  199.9 5.7 %copy-start.3 = (bf16[64,44,140]{2,1,0:T(8,128)(2,1)S(1)}, bf16[64,44,140]{2,1,0:T(8,128)(2,1)}, u32[]{:S(2)}) copy-start(bf16[64,44,140]{2,1,0:T(8,128)(2,1)} %fusion.15) | copy-start | bytes 2365444
  213.7 0.9 copy-start.14
  213.7 0.9 copy-start.31
  219.7 0.9 copy-start.12
  219.7 0.9 copy-start.30
  225.9 5.8 %copy-start.5 = (bf16[64,40,136]{2,1,0:T(8,128)(2,1)S(1)}, bf16[64,40,136]{2,1,0:T(8,128)(2,1)}, u32[]{:S(2)}) copy-start(bf16[64,40,136]{2,1,0:T(8,128)(2,1)} %fusion.35) | copy-start | bytes 2088964
  242.4 0.9 copy-start.10
  242.4 0.9 copy-start.29
  248.2 0.9 copy-start.8
  248.2 0.9 copy-start.28
  259.1 27.4 %collective-permute-start.10 = (bf16[64,8,8]{2,1,0:T(8,128)(2,1)S(1)}, bf16[64,8,8]{2,1,0:T(8,128)(2,1)S(1)}, u32[]{:S(2)}, u32[]{:S(2)}) collective-permute-start(bf16[64,8,8]{2,1,0:T(8,128)(2,1)S(1)} %get-tuple-element.18), channel_id=1, source_target_pairs={{1,16},{2,17},{3,18},{4,19},{5,20},{6,21},{7,22},{8,23},{9,24},{10... | collective-permute-start | bytes 24584 | tf_op jit(solution)/shard_map/ppermute | solution.py:33
  267.3 57.9 %collective-permute-start.14 = (bf16[64,8,128]{2,1,0:T(8,128)(2,1)S(1)}, bf16[64,8,128]{2,1,0:T(8,128)(2,1)S(1)}, u32[]{:S(2)}, u32[]{:S(2)}) collective-permute-start(bf16[64,8,128]{2,1,0:T(8,128)(2,1)S(1)} %get-tuple-element.20), channel_id=1, source_target_pairs={{16,0},{17,1},{18,2},{19,3},{20,4},{21,5},{22,6},{23,7},{24,8},{25... | collective-permute-start | bytes 393224 | tf_op jit(solution)/shard_map/ppermute | solution.py:33
  269.2 56.0 %collective-permute-start.9 = (bf16[64,8,128]{2,1,0:T(8,128)(2,1)S(1)}, bf16[64,8,128]{2,1,0:T(8,128)(2,1)S(1)}, u32[]{:S(2)}, u32[]{:S(2)}) collective-permute-start(bf16[64,8,128]{2,1,0:T(8,128)(2,1)S(1)} %get-tuple-element.19), channel_id=1, source_target_pairs={{0,16},{1,17},{2,18},{3,19},{4,20},{5,21},{6,22},{7,23},{8,24},{9,... | collective-permute-start | bytes 393224 | tf_op jit(solution)/shard_map/ppermute | solution.py:33
  279.1 46.1 %collective-permute-start.11 = (bf16[64,32,8]{2,1,0:T(8,128)(2,1)S(1)}, bf16[64,32,8]{2,1,0:T(8,128)(2,1)S(1)}, u32[]{:S(2)}, u32[]{:S(2)}) collective-permute-start(bf16[64,32,8]{2,1,0:T(8,128)(2,1)S(1)} %get-tuple-element.21), channel_id=1, source_target_pairs={{0,1},{1,2},{2,3},{3,4},{4,5},{5,6},{6,7},{7,8},{8,9},{9,10},{10,1... | collective-permute-start | bytes 98312 | tf_op jit(solution)/shard_map/ppermute | solution.py:33
  283.7 41.5 %collective-permute-start.12 = (bf16[64,32,8]{2,1,0:T(8,128)(2,1)S(1)}, bf16[64,32,8]{2,1,0:T(8,128)(2,1)S(1)}, u32[]{:S(2)}, u32[]{:S(2)}) collective-permute-start(bf16[64,32,8]{2,1,0:T(8,128)(2,1)S(1)} %get-tuple-element.22), channel_id=1, source_target_pairs={{1,0},{2,1},{3,2},{4,3},{5,4},{6,5},{7,6},{8,7},{9,8},{10,9},{11,1... | collective-permute-start | bytes 98312 | tf_op jit(solution)/shard_map/ppermute | solution.py:33
  286.5 16.3 %collective-permute-start.13 = (bf16[64,8,8]{2,1,0:T(8,128)(2,1)S(1)}, bf16[64,8,8]{2,1,0:T(8,128)(2,1)S(1)}, u32[]{:S(2)}, u32[]{:S(2)}) collective-permute-start(bf16[64,8,8]{2,1,0:T(8,128)(2,1)S(1)} %get-tuple-element.17), channel_id=1, source_target_pairs={{16,1},{17,2},{18,3},{19,4},{20,5},{21,6},{22,7},{23,8},{24,9},{25... | collective-permute-start | bytes 24584 | tf_op jit(solution)/shard_map/ppermute | solution.py:33
  302.9 13.9 %collective-permute-start.15 = (bf16[64,8,8]{2,1,0:T(8,128)(2,1)S(1)}, bf16[64,8,8]{2,1,0:T(8,128)(2,1)S(1)}, u32[]{:S(2)}, u32[]{:S(2)}) collective-permute-start(bf16[64,8,8]{2,1,0:T(8,128)(2,1)S(1)} %get-tuple-element.16), channel_id=1, source_target_pairs={{17,0},{18,1},{19,2},{20,3},{21,4},{22,5},{23,6},{24,7},{25,8},{26... | collective-permute-start | bytes 24584 | tf_op jit(solution)/shard_map/ppermute | solution.py:33
  316.8 8.4 %collective-permute-start.8 = (bf16[64,8,8]{2,1,0:T(8,128)(2,1)S(1)}, bf16[64,8,8]{2,1,0:T(8,128)(2,1)S(1)}, u32[]{:S(2)}, u32[]{:S(2)}) collective-permute-start(bf16[64,8,8]{2,1,0:T(8,128)(2,1)S(1)} %get-tuple-element.15), channel_id=1, source_target_pairs={{0,17},{1,18},{2,19},{3,20},{4,21},{5,22},{6,23},{7,24},{8,25},{9,... | collective-permute-start | bytes 24584 | tf_op jit(solution)/shard_map/ppermute | solution.py:33
  330.9 2.3 copy-start.23
  340.9 0.9 copy-start.21
  366.7 0.9 copy-start.19
  374.5 0.9 copy-start.17
  381.8 5.7 %copy-start.2 = (bf16[64,44,140]{2,1,0:T(8,128)(2,1)S(1)}, bf16[64,44,140]{2,1,0:T(8,128)(2,1)}, u32[]{:S(2)}) copy-start(bf16[64,44,140]{2,1,0:T(8,128)(2,1)} %fusion.13) | copy-start | bytes 2365444
  395.6 0.9 copy-start.15
  401.6 0.9 copy-start.13
  407.8 5.8 %copy-start.4 = (bf16[64,40,136]{2,1,0:T(8,128)(2,1)S(1)}, bf16[64,40,136]{2,1,0:T(8,128)(2,1)}, u32[]{:S(2)}) copy-start(bf16[64,40,136]{2,1,0:T(8,128)(2,1)} %fusion.31) | copy-start | bytes 2088964
  424.2 0.9 copy-start.11
  430.2 0.9 copy-start.9
  434.3 7.3 %copy-start.1 = (bf16[1,576,2048]{2,1,0:T(8,128)(2,1)S(1)}, bf16[1,576,2048]{2,1,0:T(8,128)(2,1)}, u32[]{:S(2)}) copy-start(bf16[1,576,2048]{2,1,0:T(8,128)(2,1)} %param.10) | copy-start | bytes 7077892
